TPU v7x, 32 devices: a whole 2x2x4 slice. The times are simulated.
32 devices in a mesh: fsdp: 4 (over y, x), seq: 8 (over z, core).
Axes of the slice: x: 2, y: 2, z: 4, core: 2. Of those that a mesh axis runs over, the one named last changes fastest.
Arguments:
- events: bfloat16 [4, 1024, 2048], P('fsdp', 'seq'), may hold values from -6 to 6
- type_ids: int32 [4, 1024], P('fsdp', 'seq'), may hold values from 0 to 255
- type_table: bfloat16 [256, 2048], P('fsdp'), may hold values from -6 to 6
- norm_gain: float32 [2048], replicated, may hold values from 0.25 to 1.75
- kernel: bfloat16 [2048, 1152], P('fsdp'), may hold values from -0.1875 to 0.1875
- upstream: bfloat16 [4, 1024, 2048], P('fsdp', 'seq'), may hold values from -6 to 6
Outputs:
- input_grad: bfloat16 [4, 1024, 2048], P('fsdp', 'seq')
- table_grad: float32 [256, 2048], P(('fsdp', 'seq'))
- gain_grad: float32 [2048], P(('fsdp', 'seq'))
- kernel_grad: float32 [2048, 1152], P('seq')
All inputs are finite; a program needn't handle non-finite values.
Results may differ from a plain program's by a relative error of at most 0.0053.
Values may be sent and summed in bfloat16 or wider, within the bound.
No kernel may reach another device: no remote copies, remote signals or barrier semaphores. Data moves between devices by JAX's collectives and lax.ppermute only.
A program may use at most 128 MiB of HBM per device.

v0:
```python
import jax
import jax.numpy as jnp
from jax import lax
from jax.sharding import PartitionSpec as P

GROUPS = 16
KERNEL = 9


def with_halo(cells, sides, width):
    for axis, dim in sides:
        count = lax.axis_size(axis)
        ends = count - 1
        head = lax.slice_in_dim(cells, 0, width, axis=dim)
        tail = lax.slice_in_dim(cells, cells.shape[dim] - width, cells.shape[dim], axis=dim)
        cells = jnp.concatenate(
            [
                lax.ppermute(tail, axis, [(i, (i + 1) % count) for i in range(ends)]),
                cells,
                lax.ppermute(head, axis, [((i + 1) % count, i) for i in range(ends)]),
            ],
            axis=dim,
        )
    return cells


def from_partner(value, axis, apart):
    mask = 2**apart
    pairs = [(source, source ^ mask) for source in range(lax.axis_size(axis))]
    return lax.ppermute(value, axis, pairs)


def gather_rows(block, axis):
    count = lax.axis_size(axis)
    return lax.all_to_all(jnp.tile(block, (count, 1)), axis, 0, 0, tiled=True)


def sum_rows(block, axis):
    count = lax.axis_size(axis)
    parts = block.reshape(count, block.shape[0] // count, *block.shape[1:])
    return lax.all_to_all(parts, axis, 0, 0, tiled=True).sum(axis=0)


def psum_rows(block, axis):
    return gather_rows(sum_rows(block, axis), axis)


def scatter_terms(table_term, gain_term):
    fsdp = lax.axis_size("fsdp")
    seq = lax.axis_size("seq")
    types, width = table_term.shape
    wide = width // fsdp
    gain_rows = (
        jnp.zeros((fsdp, 1, width), jnp.float32).at[:, 0, :wide].set(gain_term.reshape(fsdp, wide))
    )
    first = jnp.concatenate([table_term.reshape(fsdp, types // fsdp, width), gain_rows], axis=1)
    first = lax.all_to_all(first, "fsdp", 0, 0, tiled=True).sum(axis=0)
    rows = types // fsdp
    narrow = wide // seq
    gain_rows = (
        jnp.zeros((seq, 1, width), jnp.float32)
        .at[:, 0, :narrow]
        .set(first[rows, :wide].reshape(seq, narrow))
    )
    second = jnp.concatenate([first[:rows].reshape(seq, rows // seq, width), gain_rows], axis=1)
    second = lax.all_to_all(second, "seq", 0, 0, tiled=True).sum(axis=0)
    return (second[: rows // seq], second[rows // seq, :narrow])


def body(events, type_ids, type_table, norm_gain, kernel, upstream):
    length = events.shape[1]
    width = events.shape[2]
    chans = width // GROUPS
    half = KERNEL // 2
    seq_count = lax.axis_size("seq")
    total = length * seq_count * lax.axis_size("fsdp")
    scale = 1.0 / jnp.sqrt(jnp.float32(total))
    table = gather_rows(type_table, "fsdp")
    onehot = (type_ids[0][:, None] == jnp.arange(table.shape[0], dtype=jnp.int32)[None, :]).astype(
        jnp.bfloat16
    )
    mixed = events[0].astype(jnp.float32) + jnp.dot(
        onehot, table, preferred_element_type=jnp.float32
    )
    inv = lax.rsqrt(jnp.mean(mixed * mixed, axis=-1, keepdims=True) + 1e-06)
    normed = (mixed * inv * norm_gain).astype(jnp.bfloat16)
    padded = with_halo(normed, (("seq", 0),), half)
    padded = padded.reshape(length + 2 * half, GROUPS, chans)
    weights = lax.all_gather(kernel, "fsdp", axis=0, tiled=True).reshape(
        GROUPS, chans, KERNEL, chans
    )
    conv = jnp.zeros((length, GROUPS, chans), jnp.float32)
    for k in range(KERNEL):
        conv = conv + jnp.einsum(
            "tgc,goc->tgo",
            padded[k : k + length],
            weights[:, :, k, :],
            preferred_element_type=jnp.float32,
        )
    up_float = upstream[0].astype(jnp.float32)
    sig = jax.nn.sigmoid(conv)
    dconv = (up_float.reshape(length, GROUPS, chans) * sig * (1.0 + conv * (1.0 - sig))).astype(
        jnp.bfloat16
    )
    dflat = dconv.reshape(length, width)
    dpad = with_halo(dflat, (("seq", 0),), half)
    dpad = dpad.reshape(length + 2 * half, GROUPS, chans)
    dnormed = jnp.zeros((length, GROUPS, chans), jnp.float32)
    for k in range(KERNEL):
        dnormed = dnormed + jnp.einsum(
            "tgo,goc->tgc",
            dpad[2 * half - k : 2 * half - k + length],
            weights[:, :, k, :],
            preferred_element_type=jnp.float32,
        )
    slice_width = width // seq_count
    normed_slice, dconv_slice = (
        lax.all_to_all(normed, "seq", split_axis=1, concat_axis=0, tiled=True),
        lax.all_to_all(dflat, "seq", split_axis=1, concat_axis=0, tiled=True),
    )
    whole = normed_slice.shape[0]
    if slice_width < chans:
        spread = chans // slice_width
        position = lax.axis_index("seq")
        group_rows = normed_slice
        for bit in range(spread.bit_length() - 1):
            partner = from_partner(group_rows, "seq", bit)
            lower = position >> bit & 1 == 0
            group_rows = jnp.where(
                lower,
                jnp.concatenate([group_rows, partner], axis=1),
                jnp.concatenate([partner, group_rows], axis=1),
            )
        group_in = group_rows.reshape(whole, 1, chans)
        group_out = dconv_slice.reshape(whole, 1, slice_width)
    else:
        local_groups = slice_width // chans
        group_in = normed_slice.reshape(whole, local_groups, chans)
        group_out = dconv_slice.reshape(whole, local_groups, chans)
    group_pad = jnp.pad(group_in, ((half, half), (0, 0), (0, 0)))
    kterms = []
    for k in range(KERNEL):
        kterms.append(
            jnp.einsum(
                "tgo,tgc->goc",
                group_out,
                group_pad[k : k + whole],
                preferred_element_type=jnp.float32,
            )
        )
    kernel_part = jnp.stack(kterms, axis=2).reshape(slice_width, KERNEL * chans) * scale
    kernel_grad = psum_rows(kernel_part, "fsdp")
    dnormed = dnormed.reshape(length, width)
    gain_term = jnp.sum(dnormed * mixed * inv, axis=0) * scale
    scaled = norm_gain * dnormed
    dmixed = inv * scaled - mixed * inv * inv * inv * jnp.mean(
        scaled * mixed, axis=-1, keepdims=True
    )
    input_grad = (up_float + dmixed).astype(jnp.bfloat16)
    table_term = (
        lax.dot_general(
            onehot, input_grad, (((0,), (0,)), ((), ())), preferred_element_type=jnp.float32
        )
        * scale
    )
    table_grad, gain_grad = scatter_terms(table_term, gain_term)
    return (input_grad[None], table_grad, gain_grad, kernel_grad)


def solution(mesh):
    return jax.shard_map(
        body,
        mesh=mesh,
        in_specs=(
            P("fsdp", "seq", None),
            P("fsdp", "seq"),
            P("fsdp", None),
            P(),
            P("fsdp", None),
            P("fsdp", "seq", None),
        ),
        out_specs=(
            P("fsdp", "seq", None),
            P(("fsdp", "seq"), None),
            P(("fsdp", "seq")),
            P("seq", None),
        ),
        check_vma=False,
    )
```

profile of v0, /device:TPU:0, one launch (start us, length us, event | category | flops | bytes accessed | tf_op | source)
XLA Modules:
  0.0 257.1 jit_solution(17122217566961818963)
XLA Ops:
  7.2 0.7 all-gather.2.cloned.1.call-update
  8.3 23.8 %all_to_all.65 = bf16[4,64,2048]{2,1,0:T(8,128)(2,1)S(1)} all-to-all(bf16[4,64,2048]{2,1,0:T(8,128)(2,1)S(1)} %tile.4), channel_id=1, replica_groups=mesh['fsdp'=4,'seq'=8] {'fsdp'}, dimensions={0} | all-to-all | bytes 2097152 | tf_op jit(solution)/shard_map/all_to_all | solution.py:35
  32.0 0.4 multiply_reduce_fusion.2
  32.9 1.0 copy.290
  33.9 5.2 %all-to-all-start.4 = ((bf16[128,8,256]{0,2,1:T(8,128)(2,1)}), bf16[128,8,256]{0,2,1:T(8,128)(2,1)S(1)}, u32[]{:S(2)}, u32[]{:S(2)}) async-start(bf16[128,8,256]{0,2,1:T(8,128)(2,1)} %bitcast.35), calls=%async_computation.4 | async-start | bytes 1048576 | tf_op jit(solution)/shard_map/all_to_all | solution.py:118
  39.1 2.4 collective-permute-start
  41.5 1.3 collective-permute-start.1
  42.9 1.2 copy.314
  44.0 1.6 collective-permute-done.1
  45.7 2.7 %fusion.52 = (bf16[16,16,8,128]{3,2,1,0:T(8,128)(2,1)}, bf16[16,16,8,128]{3,2,1,0:T(8,128)(2,1)}, bf16[16,16,8,128]{3,2,1,0:T(8,128)(2,1)}, bf16[16,16,8,128]{3,...) fusion(bf16[4,2048]{1,0:T(4,128)(2,1)S(1)} %collective-permute-, ...), kind=kLoop, calls=%fused_computation.112 | loop fusion | flops 8388608 | bytes 4751360
  48.3 6.1 %all-to-all-done.4 = bf16[128,8,256]{0,2,1:T(8,128)(2,1)S(1)} async-done(((bf16[128,8,256]{0,2,1:T(8,128)(2,1)}), bf16[128,8,256]{0,2,1:T(8,128)(2,1)S(1)}, u32[]{:S(2)}, u32[]{:S(2)}) %all-to-all-start.4) | async-done | bytes 524320 | tf_op jit(solution)/shard_map/all_to_all | solution.py:118
  55.0 1.0 copy.268
  56.0 17.2 %all-gather.2.cloned.1.call-done = bf16[2048,1152]{1,0:T(8,128)(2,1)} async-done(((bf16[512,1152]{1,0:T(8,128)(2,1)}), bf16[2048,1152]{1,0:T(8,128)(2,1)}) %all-gather.2.cloned.1.call-update) | async-done | bytes 4718608 | tf_op jit(solution)/shard_map/all_gather | solution.py:89
  73.1 10.5 %reshape.199 = bf16[16,128,9,128]{3,2,1,0:T(8,128)(2,1)} reshape(bf16[2048,1152]{1,0:T(8,128)(2,1)} %all-gather.2.cloned.1.call-done) | data formatting | bytes 9437184 | tf_op jit(solution)/shard_map/reshape | solution.py:89
  83.6 19.7 %fusion.82 = (bf16[16,128,1,128]{3,2,1,0:T(2,128)(2,1)S(1)}, bf16[16,128,1,128]{3,2,1,0:T(2,128)(2,1)S(1)}, bf16[16,128,1,128]{3,2,1,0:T(2,128)(2,1)S(1)}, bf16[...) fusion(bf16[16,128,9,128]{3,2,1,0:T(8,128)(2,1)} %reshape.199), kind=kLoop, calls=%fused_computation.160 | loop fusion | bytes 9437184 | tf_op jit(solution)/shard_map/slice | solution.py:97
  103.5 0.5 fusion.49
  103.9 0.9 copy-done.24
  104.9 0.5 convolution_add_fusion.15
  105.4 0.9 copy-done.23
  106.3 0.5 convolution_add_fusion.14
  106.8 0.7 copy-done.22
  107.5 0.5 convolution_add_fusion.13
  108.0 0.5 convolution_add_fusion.12
  108.5 0.5 copy-done.21
  109.0 0.5 convolution_add_fusion.11
  109.5 0.5 copy-done.20
  110.1 0.5 convolution_add_fusion.10
  110.6 0.5 convolution_add_fusion.9
  111.1 0.7 copy-done.27
  111.9 0.8 fusion.14
  113.1 1.3 collective-permute-start.2
  114.4 1.1 copy.253
  115.5 3.9 %collective-permute-start.3 = (bf16[4,2048]{0,1:T(8,128)(2,1)}, bf16[4,2048]{0,1:T(8,128)(2,1)}, u32[]{:S(2)}, u32[]{:S(2)}) collective-permute-start(bf16[4,2048]{0,1:T(8,128)(2,1)} %copy.253), channel_id=1, source_target_pairs={{0,1},{1,2},{2,3},{3,4},{4,5},{5,6},{6,7},{8,9},{9,10},{10,11},{11... | collective-permute-start | bytes 49160 | tf_op jit(solution)/shard_map/ppermute | solution.py:18
  119.3 2.7 %fusion.63 = f32[16,128,128]{1,2,0:T(8,128)} fusion(bf16[128,16,128]{2,0,1:T(8,128)(2,1)S(1)} %fusion.14, bf16[16,128,1,128]{3,2,1,0:T(2,128)(2,1)} %copy-done.12), kind=kOutput, calls=%fused_computation.133 | convolution fusion | flops 67108864 | bytes 2097152 | tf_op jit(solution)/shard_map/tgo,goc->tgc/dot_general | solution.py:110
  122.0 1.1 copy.242
  123.1 4.6 %all-to-all-start.3 = ((bf16[128,8,256]{0,2,1:T(8,128)(2,1)}), bf16[128,8,256]{0,2,1:T(8,128)(2,1)}, u32[]{:S(2)}, u32[]{:S(2)}) async-start(bf16[128,8,256]{0,2,1:T(8,128)(2,1)} %bitcast.33), calls=%async_computation.3 | async-start | bytes 1048576 | tf_op jit(solution)/shard_map/all_to_all | solution.py:119
  127.7 6.5 %pad_maximum_fusion = (bf16[128,2048]{0,1:T(8,128)(2,1)S(1)}, bf16[128,2048]{0,1:T(8,128)(2,1)S(1)}, bf16[128,2048]{0,1:T(8,128)(2,1)S(1)}, bf16[128,2048]{0,1:T...) fusion(bf16[128,2048]{0,1:T(8,128)(2,1)} %bitcast.14, ...), kind=kLoop, calls=%fused_computation.109 | loop fusion | flops 8388608 | bytes 4751360 | tf_op jit(solution)/shard_map/concatenate | solution.py:16
  134.6 0.8 copy-done.9
  135.8 0.9 copy-done.7
  137.0 0.9 copy-done.14
  138.5 0.9 copy-done.5
  139.8 0.9 copy-done.3
  141.4 0.9 copy-done.17
  143.2 0.7 copy-done.19
  144.4 0.5 convolution_multiply_fusion
  145.2 1.7 select_maximum_fusion
  146.8 3.6 %all-to-all-start.1 = ((f32[4,65,2048]{2,1,0:T(8,128)}), f32[4,65,2048]{2,1,0:T(8,128)S(1)}, u32[]{:S(2)}, u32[]{:S(2)}) async-start(f32[4,65,2048]{2,1,0:T(8,128)} %select_maximum_fusion), calls=%async_computation.1 | async-start | bytes 4718592 | tf_op jit(solution)/shard_map/all_to_all | solution.py:57
  150.5 1.4 copy.265
  152.1 1.4 fusion.10
  156.6 2.1 copy.270
  158.7 2.5 mul.133
  161.2 17.9 %all-to-all-done.1 = f32[4,65,2048]{2,1,0:T(8,128)S(1)} async-done(((f32[4,65,2048]{2,1,0:T(8,128)}), f32[4,65,2048]{2,1,0:T(8,128)S(1)}, u32[]{:S(2)}, u32[]{:S(2)}) %all-to-all-start.1) | async-done | bytes 2129952 | tf_op jit(solution)/shard_map/all_to_all | solution.py:57
  179.1 4.3 %all-to-all-start.5 = ((f32[4,64,1152]{2,1,0:T(8,128)}), f32[4,64,1152]{2,1,0:T(8,128)}, u32[]{:S(2)}, u32[]{:S(2)}) async-start(f32[4,64,1152]{2,1,0:T(8,128)} %mul.133), calls=%async_computation.5 | async-start | bytes 2359296 | tf_op jit(solution)/shard_map/all_to_all | solution.py:41
  183.7 1.1 select_maximum_fusion.1
  184.8 13.9 %all-to-all-done.5 = f32[4,64,1152]{2,1,0:T(8,128)} async-done(((f32[4,64,1152]{2,1,0:T(8,128)}), f32[4,64,1152]{2,1,0:T(8,128)}, u32[]{:S(2)}, u32[]{:S(2)}) %all-to-all-start.5) | async-done | bytes 1179680 | tf_op jit(solution)/shard_map/all_to_all | solution.py:41
  198.6 4.3 %all-to-all-start.2 = ((f32[8,9,2048]{2,1,0:T(8,128)}), f32[8,9,2048]{2,1,0:T(8,128)S(1)}, u32[]{:S(2)}, u32[]{:S(2)}) async-start(f32[8,9,2048]{2,1,0:T(8,128)} %select_maximum_fusion.1), calls=%async_computation.2 | async-start | bytes 2097152 | tf_op jit(solution)/shard_map/all_to_all | solution.py:66
  203.0 1.4 reduce_sum.59
  204.3 25.2 %all-to-all-done.2 = f32[8,9,2048]{2,1,0:T(8,128)S(1)} async-done(((f32[8,9,2048]{2,1,0:T(8,128)}), f32[8,9,2048]{2,1,0:T(8,128)S(1)}, u32[]{:S(2)}, u32[]{:S(2)}) %all-to-all-start.2) | async-done | bytes 589856 | tf_op jit(solution)/shard_map/all_to_all | solution.py:66
  229.6 1.1 tile.5
  230.6 3.5 %all-to-all-start.6 = ((f32[4,64,1152]{2,1,0:T(8,128)}), f32[4,64,1152]{2,1,0:T(8,128)S(1)}, u32[]{:S(2)}, u32[]{:S(2)}) async-start(f32[4,64,1152]{2,1,0:T(8,128)} %tile.5), calls=%async_computation.6 | async-start | bytes 2359296 | tf_op jit(solution)/shard_map/all_to_all | solution.py:35
  234.3 0.6 slice.354
  234.9 0.5 slice_bitcast_fusion.3
  235.4 13.9 %all-to-all-done.6 = f32[4,64,1152]{2,1,0:T(8,128)S(1)} async-done(((f32[4,64,1152]{2,1,0:T(8,128)}), f32[4,64,1152]{2,1,0:T(8,128)S(1)}, u32[]{:S(2)}, u32[]{:S(2)}) %all-to-all-start.6) | async-done | bytes 1179680 | tf_op jit(solution)/shard_map/all_to_all | solution.py:35
  249.3 1.0 copy.392
  (97 shorter events, 10.0 us)
Async XLA Ops:
  7.2 1.0 copy-start.31
  7.2 66.0 %all-gather.2.cloned.1.call-start = ((), (), s32[]{:S(2)}) async-start(), calls=%async_computation.7 | async-start | bytes 5898240 | tf_op jit(solution)/shard_map/all_gather | solution.py:89
  8.2 23.8 %copy-start.28 = (bf16[1,128,2048]{2,1,0:T(8,128)(2,1)S(1)}, bf16[1,128,2048]{2,1,0:T(8,128)(2,1)}, u32[]{:S(2)}) copy-start(bf16[1,128,2048]{2,1,0:T(8,128)(2,1)} %param.10) | copy-start | bytes 1572868
  8.2 23.8 %copy-start.33 = (s32[1,128]{1,0:T(1,128)S(1)}, s32[1,128]{1,0:T(1,128)}, u32[]{:S(2)}) copy-start(s32[1,128]{1,0:T(1,128)} %param.11) | copy-start | bytes 1540
  32.0 0.7 copy-start.32
  32.9 9.9 %copy-start.18 = (bf16[1,128,2048]{2,1,0:T(8,128)(2,1)S(1)}, bf16[1,128,2048]{2,1,0:T(8,128)(2,1)}, u32[]{:S(2)}) copy-start(bf16[1,128,2048]{2,1,0:T(8,128)(2,1)} %param.15) | copy-start | bytes 1572868
  33.9 20.5 %all-to-all-start.4 = ((bf16[128,8,256]{0,2,1:T(8,128)(2,1)}), bf16[128,8,256]{0,2,1:T(8,128)(2,1)S(1)}, u32[]{:S(2)}, u32[]{:S(2)}) async-start(bf16[128,8,256]{0,2,1:T(8,128)(2,1)} %bitcast.35), calls=%async_computation.4 | async-start | bytes 1048576 | tf_op jit(solution)/shard_map/all_to_all | solution.py:118
  39.1 5.0 %collective-permute-start = (bf16[4,2048]{1,0:T(4,128)(2,1)S(1)}, bf16[4,2048]{1,0:T(4,128)(2,1)S(1)}, u32[]{:S(2)}, u32[]{:S(2)}) collective-permute-start(bf16[4,2048]{1,0:T(4,128)(2,1)S(1)} %get-tuple-element.66), channel_id=1, source_target_pairs={{0,1},{1,2},{2,3},{3,4},{4,5},{5,6},{6,7},{8,9},{9,10},{10,11},{11... | collective-permute-start | bytes 49160 | tf_op jit(solution)/shard_map/ppermute | solution.py:18
  41.5 4.2 %collective-permute-start.1 = (bf16[4,2048]{1,0:T(4,128)(2,1)S(1)}, bf16[4,2048]{1,0:T(4,128)(2,1)S(1)}, u32[]{:S(2)}, u32[]{:S(2)}) collective-permute-start(bf16[4,2048]{1,0:T(4,128)(2,1)S(1)} %get-tuple-element.65), channel_id=1, source_target_pairs={{1,0},{2,1},{3,2},{4,3},{5,4},{6,5},{7,6},{9,8},{10,9},{11,10},{12... | collective-permute-start | bytes 49160 | tf_op jit(solution)/shard_map/ppermute | solution.py:20
  55.0 28.6 %copy-start = (bf16[1024,2,128]{0,2,1:T(8,128)(2,1)}, bf16[1024,2,128]{0,2,1:T(8,128)(2,1)S(1)}, u32[]{:S(2)}) copy-start(bf16[1024,2,128]{0,2,1:T(8,128)(2,1)S(1)} %reshape.195) | copy-start | bytes 1572868
  83.6 19.8 %copy-start.25 = (bf16[16,16,8,128]{3,2,1,0:T(8,128)(2,1)S(1)}, bf16[16,16,8,128]{3,2,1,0:T(8,128)(2,1)}, u32[]{:S(2)}) copy-start(bf16[16,16,8,128]{3,2,1,0:T(8,128)(2,1)} %get-tuple-element.63) | copy-start | bytes 1572868
  103.4 2.0 copy-start.8
  103.4 2.0 copy-start.10
  103.4 2.0 copy-start.6
  103.4 3.4 %copy-start.13 = (bf16[16,128,1,128]{3,2,1,0:T(2,128)(2,1)}, bf16[16,128,1,128]{3,2,1,0:T(2,128)(2,1)S(1)}, u32[]{:S(2)}) copy-start(bf16[16,128,1,128]{3,2,1,0:T(2,128)(2,1)S(1)} %get-tuple-element.35) | copy-start | bytes 1572868
  103.4 4.6 %copy-start.12 = (bf16[16,128,1,128]{3,2,1,0:T(2,128)(2,1)}, bf16[16,128,1,128]{3,2,1,0:T(2,128)(2,1)S(1)}, u32[]{:S(2)}) copy-start(bf16[16,128,1,128]{3,2,1,0:T(2,128)(2,1)S(1)} %get-tuple-element.34) | copy-start | bytes 1572868
  103.4 5.1 %copy-start.4 = (bf16[16,128,1,128]{3,2,1,0:T(2,128)(2,1)}, bf16[16,128,1,128]{3,2,1,0:T(2,128)(2,1)S(1)}, u32[]{:S(2)}) copy-start(bf16[16,128,1,128]{3,2,1,0:T(2,128)(2,1)S(1)} %get-tuple-element.33) | copy-start | bytes 1572868
  103.4 6.1 %copy-start.2 = (bf16[16,128,1,128]{3,2,1,0:T(2,128)(2,1)}, bf16[16,128,1,128]{3,2,1,0:T(2,128)(2,1)S(1)}, u32[]{:S(2)}) copy-start(bf16[16,128,1,128]{3,2,1,0:T(2,128)(2,1)S(1)} %get-tuple-element.32) | copy-start | bytes 1572868
  103.4 7.6 %copy-start.16 = (bf16[16,128,1,128]{3,2,1,0:T(2,128)(2,1)}, bf16[16,128,1,128]{3,2,1,0:T(2,128)(2,1)S(1)}, u32[]{:S(2)}) copy-start(bf16[16,128,1,128]{3,2,1,0:T(2,128)(2,1)S(1)} %get-tuple-element.30) | copy-start | bytes 1572868
  103.4 1.4 copy-start.24
  104.9 1.4 copy-start.23
  106.3 1.2 copy-start.22
  108.0 1.0 copy-start.21
  109.0 1.0 copy-start.20
  110.5 1.2 copy-start.27
  110.6 1.3 copy-start.29
  113.1 14.5 %collective-permute-start.2 = (bf16[4,2048]{0,1:T(8,128)(2,1)S(1)}, bf16[4,2048]{0,1:T(8,128)(2,1)}, u32[]{:S(2)}, u32[]{:S(2)}) collective-permute-start(bf16[4,2048]{0,1:T(8,128)(2,1)S(1)} %copy.243), channel_id=1, source_target_pairs={{1,0},{2,1},{3,2},{4,3},{5,4},{6,5},{7,6},{9,8},{10,9},{11,10},{12... | collective-permute-start | bytes 49160 | tf_op jit(solution)/shard_map/ppermute | solution.py:20
  115.5 12.2 %collective-permute-start.3 = (bf16[4,2048]{0,1:T(8,128)(2,1)}, bf16[4,2048]{0,1:T(8,128)(2,1)}, u32[]{:S(2)}, u32[]{:S(2)}) collective-permute-start(bf16[4,2048]{0,1:T(8,128)(2,1)} %copy.253), channel_id=1, source_target_pairs={{0,1},{1,2},{2,3},{3,4},{4,5},{5,6},{6,7},{8,9},{9,10},{10,11},{11... | collective-permute-start | bytes 49160 | tf_op jit(solution)/shard_map/ppermute | solution.py:18
  123.1 23.8 %all-to-all-start.3 = ((bf16[128,8,256]{0,2,1:T(8,128)(2,1)}), bf16[128,8,256]{0,2,1:T(8,128)(2,1)}, u32[]{:S(2)}, u32[]{:S(2)}) async-start(bf16[128,8,256]{0,2,1:T(8,128)(2,1)} %bitcast.33), calls=%async_computation.3 | async-start | bytes 1048576 | tf_op jit(solution)/shard_map/all_to_all | solution.py:119
  127.7 6.5 %copy-start.11 = (bf16[16,128,1,128]{3,2,1,0:T(2,128)(2,1)S(1)}, bf16[16,128,1,128]{3,2,1,0:T(2,128)(2,1)}, u32[]{:S(2)}) copy-start(bf16[16,128,1,128]{3,2,1,0:T(2,128)(2,1)} %copy-done.10) | copy-start | bytes 1572868
  134.2 1.2 copy-start.9
  135.4 1.2 copy-start.7
  136.6 1.2 copy-start.14
  136.6 1.5 copy-start.15
  138.2 1.2 copy-start.5
  139.4 1.2 copy-start.3
  141.0 1.2 copy-start.17
  142.9 1.0 copy-start.19
  144.4 0.8 copy-start.26
  146.8 32.2 %all-to-all-start.1 = ((f32[4,65,2048]{2,1,0:T(8,128)}), f32[4,65,2048]{2,1,0:T(8,128)S(1)}, u32[]{:S(2)}, u32[]{:S(2)}) async-start(f32[4,65,2048]{2,1,0:T(8,128)} %select_maximum_fusion), calls=%async_computation.1 | async-start | bytes 4718592 | tf_op jit(solution)/shard_map/all_to_all | solution.py:57
  152.1 1.4 copy-start.30
  153.9 1.0 copy-start.1
  179.1 19.5 %all-to-all-start.5 = ((f32[4,64,1152]{2,1,0:T(8,128)}), f32[4,64,1152]{2,1,0:T(8,128)}, u32[]{:S(2)}, u32[]{:S(2)}) async-start(f32[4,64,1152]{2,1,0:T(8,128)} %mul.133), calls=%async_computation.5 | async-start | bytes 2359296 | tf_op jit(solution)/shard_map/all_to_all | solution.py:41
  198.6 30.9 %all-to-all-start.2 = ((f32[8,9,2048]{2,1,0:T(8,128)}), f32[8,9,2048]{2,1,0:T(8,128)S(1)}, u32[]{:S(2)}, u32[]{:S(2)}) async-start(f32[8,9,2048]{2,1,0:T(8,128)} %select_maximum_fusion.1), calls=%async_computation.2 | async-start | bytes 2097152 | tf_op jit(solution)/shard_map/all_to_all | solution.py:66
  230.6 18.6 %all-to-all-start.6 = ((f32[4,64,1152]{2,1,0:T(8,128)}), f32[4,64,1152]{2,1,0:T(8,128)S(1)}, u32[]{:S(2)}, u32[]{:S(2)}) async-start(f32[4,64,1152]{2,1,0:T(8,128)} %tile.5), calls=%async_computation.6 | async-start | bytes 2359296 | tf_op jit(solution)/shard_map/all_to_all | solution.py:35
Sparse Core Ops, SparseCore 0:
  9.8 63.2 all-gather.1
where the time goes:
time: 259 us; the launch traced here: 257 us
  waiting for transfers between devices  96.4 us (37%)
  local copies, waits for them, and re-layouts  58.1 us (22%)
  starting transfers between devices  34.4 us (13%)
  blocking collectives  23.8 us (9%)
  matrix products  15.2 us (6%)
  between operations  14.7 us (6%)
  other arithmetic  14.6 us (6%)
    all_to_all x1, waiting for transfers between devices, scatter_terms(): second = lax.all_to_all(second, 'seq', 0, 0, tiled=True).sum(axis=0)  25.2 us
    all_to_all x1, blocking collectives, gather_rows(): return lax.all_to_all(jnp.tile(block, (count, 1)), axis, 0, 0, tiled=True)  23.8 us
    slice x1, local copies, waits for them, and re-layouts, body(): weights[:, :, k, :]  19.7 us
    all_to_all x1, waiting for transfers between devices, scatter_terms(): first = lax.all_to_all(first, 'fsdp', 0, 0, tiled=True).sum(axis=0)  17.9 us
    all_gather x1, waiting for transfers between devices, body(): lax.all_gather(kernel, 'fsdp', axis=0, tiled=True)  17.2 us
    unnamed x70, local copies, waits for them, and re-layouts  13.9 us
    all_to_all x1, waiting for transfers between devices, gather_rows(): return lax.all_to_all(jnp.tile(block, (count, 1)), axis, 0, 0, tiled=True)  13.9 us
    all_to_all x1, waiting for transfers between devices, sum_rows(): return lax.all_to_all(parts, axis, 0, 0, tiled=True).sum(axis=0)  13.9 us
  transfers between devices with their start and end apart: 11, of which 7 were waited for; matrix products, arithmetic and copies ran while one was open for 15% of the time, Pallas kernels for 0%

commit v1 on v0

--- a/solution.py
+++ b/solution.py
@@ -115,7 +115,10 @@
         )
     slice_width = width // seq_count
     normed_slice, dconv_slice = (
-        lax.all_to_all(normed, "seq", split_axis=1, concat_axis=0, tiled=True),
+        jnp.concatenate(
+            lax.all_to_all(jnp.stack(jnp.split(normed, lax.psum(1, "seq"), axis=1)), "seq", 0, 0),
+            axis=0,
+        ),
         lax.all_to_all(dflat, "seq", split_axis=1, concat_axis=0, tiled=True),
     )
     whole = normed_slice.shape[0]

time: 259 us -> 260 us (level)
  local copies, waits for them, and re-layouts: 58.1 us -> 65.9 us
  waiting for transfers between devices: 96.4 us -> 90.5 us
    unnamed x70 -> x79, local copies, waits for them, and re-layouts: 13.9 us -> 18.7 us
    all_gather x1, waiting for transfers between devices: 17.2 us -> 13.6 us  [body(): lax.all_gather(kernel, 'fsdp', axis=0, tiled=True)]
    all_to_all x1, waiting for transfers between devices: 13.9 us -> 11.2 us  [sum_rows(): return lax.all_to_all(parts, axis, 0, 0, tiled=True).sum(axis=0)]
  transfers between devices with their start and end apart: 11 -> 11, of which waited for: 7 -> 7; matrix products, arithmetic and copies ran while one was open for 15% -> 18% of each run, Pallas kernels for 0% -> 0%
where the time goes in v1:
time: 260 us; the launch traced here: 258 us
  waiting for transfers between devices  90.5 us (35%)
  local copies, waits for them, and re-layouts  65.9 us (25%)
  starting transfers between devices  33.7 us (13%)
  blocking collectives  23.8 us (9%)
  matrix products  15.4 us (6%)
  between operations  14.7 us (6%)
  other arithmetic  14.4 us (6%)
    all_to_all x1, waiting for transfers between devices, scatter_terms(): second = lax.all_to_all(second, 'seq', 0, 0, tiled=True).sum(axis=0)  26.5 us
    all_to_all x1, blocking collectives, gather_rows(): return lax.all_to_all(jnp.tile(block, (count, 1)), axis, 0, 0, tiled=True)  23.8 us
    slice x1, local copies, waits for them, and re-layouts, body(): weights[:, :, k, :]  19.1 us
    unnamed x79, local copies, waits for them, and re-layouts  18.7 us
    all_to_all x1, waiting for transfers between devices, scatter_terms(): first = lax.all_to_all(first, 'fsdp', 0, 0, tiled=True).sum(axis=0)  17.1 us
    all_to_all x1, waiting for transfers between devices, gather_rows(): return lax.all_to_all(jnp.tile(block, (count, 1)), axis, 0, 0, tiled=True)  13.9 us
    all_gather x1, waiting for transfers between devices, body(): lax.all_gather(kernel, 'fsdp', axis=0, tiled=True)  13.6 us
    all_to_all x1, waiting for transfers between devices, sum_rows(): return lax.all_to_all(parts, axis, 0, 0, tiled=True).sum(axis=0)  11.2 us
  transfers between devices with their start and end apart: 11, of which 7 were waited for; matrix products, arithmetic and copies ran while one was open for 18% of the time, Pallas kernels for 0%

profile of v1, /device:TPU:0, one launch (start us, length us, event | category | flops | bytes accessed | tf_op | source)
XLA Modules:
  0.0 258.2 jit_solution(15934253683774970044)
XLA Ops:
  7.2 0.7 all-gather.2.cloned.1.call-update
  8.3 23.8 %all_to_all.54 = bf16[4,64,2048]{2,1,0:T(8,128)(2,1)S(1)} all-to-all(bf16[4,64,2048]{2,1,0:T(8,128)(2,1)S(1)} %tile.4), channel_id=1, replica_groups=mesh['fsdp'=4,'seq'=8] {'fsdp'}, dimensions={0} | all-to-all | bytes 2097152 | tf_op jit(solution)/shard_map/all_to_all | solution.py:35
  32.9 0.6 fusion.79
  33.5 0.6 fusion.78
  34.2 0.6 fusion.77
  34.8 0.6 fusion.76
  35.4 0.6 fusion.75
  36.1 0.6 fusion.74
  36.7 0.6 fusion.73
  37.3 0.6 fusion.72
  38.0 5.2 %all-to-all-start.4 = ((bf16[8,128,256]{2,1,0:T(8,128)(2,1)}), bf16[8,128,256]{2,1,0:T(8,128)(2,1)S(1)}, u32[]{:S(2)}, u32[]{:S(2)}) async-start(bf16[8,128,256]{2,1,0:T(8,128)(2,1)} %fusion.72), calls=%async_computation.4 | async-start | bytes 1048576 | tf_op jit(solution)/shard_map/all_to_all | solution.py:119
  43.1 2.4 collective-permute-start
  45.6 1.3 collective-permute-start.1
  47.0 1.2 copy.259
  48.1 1.6 collective-permute-done.1
  49.8 2.8 %fusion.52 = (bf16[16,16,8,128]{3,2,1,0:T(8,128)(2,1)}, bf16[16,16,8,128]{3,2,1,0:T(8,128)(2,1)}, bf16[16,16,8,128]{3,2,1,0:T(8,128)(2,1)}, bf16[16,16,8,128]{3,...) fusion(bf16[4,2048]{1,0:T(4,128)(2,1)S(1)} %collective-permute-, ...), kind=kLoop, calls=%fused_computation.112 | loop fusion | flops 8388608 | bytes 4751360
  52.5 5.9 %all-to-all-done.4 = bf16[8,128,256]{2,1,0:T(8,128)(2,1)S(1)} async-done(((bf16[8,128,256]{2,1,0:T(8,128)(2,1)}), bf16[8,128,256]{2,1,0:T(8,128)(2,1)S(1)}, u32[]{:S(2)}, u32[]{:S(2)}) %all-to-all-start.4) | async-done | bytes 524320 | tf_op jit(solution)/shard_map/all_to_all | solution.py:119
  58.6 0.9 copy.215
  59.6 13.6 %all-gather.2.cloned.1.call-done = bf16[2048,1152]{1,0:T(8,128)(2,1)} async-done(((bf16[512,1152]{1,0:T(8,128)(2,1)}), bf16[2048,1152]{1,0:T(8,128)(2,1)}) %all-gather.2.cloned.1.call-update) | async-done | bytes 4718608 | tf_op jit(solution)/shard_map/all_gather | solution.py:89
  73.1 10.5 %reshape.191 = bf16[16,128,9,128]{3,2,1,0:T(8,128)(2,1)} reshape(bf16[2048,1152]{1,0:T(8,128)(2,1)} %all-gather.2.cloned.1.call-done) | data formatting | bytes 9437184 | tf_op jit(solution)/shard_map/reshape | solution.py:89
  83.6 19.1 %fusion.91 = (bf16[16,128,1,128]{3,2,1,0:T(2,128)(2,1)S(1)}, bf16[16,128,1,128]{3,2,1,0:T(2,128)(2,1)S(1)}, bf16[16,128,1,128]{3,2,1,0:T(2,128)(2,1)S(1)}, bf16[...) fusion(bf16[16,128,9,128]{3,2,1,0:T(8,128)(2,1)} %reshape.191), kind=kLoop, calls=%fused_computation.177 | loop fusion | bytes 9437184 | tf_op jit(solution)/shard_map/slice | solution.py:97
  103.3 0.9 copy-done.24
  104.8 0.9 copy-done.23
  106.2 0.5 copy-done.22
  108.8 0.6 copy-done.20
  110.9 0.7 copy-done.27
  111.7 0.8 fusion.14
  112.6 0.8 copy-done.14
  113.4 1.1 copy.192
  114.5 1.3 collective-permute-start.2
  115.8 1.1 copy.202
  116.8 3.9 %collective-permute-start.3 = (bf16[4,2048]{0,1:T(8,128)(2,1)}, bf16[4,2048]{0,1:T(8,128)(2,1)}, u32[]{:S(2)}, u32[]{:S(2)}) collective-permute-start(bf16[4,2048]{0,1:T(8,128)(2,1)} %copy.202), channel_id=1, source_target_pairs={{0,1},{1,2},{2,3},{3,4},{4,5},{5,6},{6,7},{8,9},{9,10},{10,11},{11... | collective-permute-start | bytes 49160 | tf_op jit(solution)/shard_map/ppermute | solution.py:18
  120.7 2.9 %fusion.63 = f32[16,128,128]{1,2,0:T(8,128)} fusion(bf16[128,16,128]{2,0,1:T(8,128)(2,1)} %copy-done.14, bf16[16,128,1,128]{3,2,1,0:T(2,128)(2,1)} %copy-done.8), kind=kOutput, calls=%fused_computation.133 | convolution fusion | flops 67108864 | bytes 2097152 | tf_op jit(solution)/shard_map/tgo,goc->tgc/dot_general | solution.py:110
  123.6 2.0 copy.191
  125.6 4.6 %all-to-all-start.3 = ((bf16[128,8,256]{0,2,1:T(8,128)(2,1)}), bf16[128,8,256]{0,2,1:T(8,128)(2,1)}, u32[]{:S(2)}, u32[]{:S(2)}) async-start(bf16[128,8,256]{0,2,1:T(8,128)(2,1)} %bitcast.33), calls=%async_computation.3 | async-start | bytes 1048576 | tf_op jit(solution)/shard_map/all_to_all | solution.py:122
  130.3 6.7 %pad_maximum_fusion = (bf16[128,2048]{0,1:T(8,128)(2,1)S(1)}, bf16[128,2048]{0,1:T(8,128)(2,1)S(1)}, bf16[128,2048]{0,1:T(8,128)(2,1)S(1)}, bf16[128,2048]{0,1:T...) fusion(bf16[128,2048]{0,1:T(8,128)(2,1)} %bitcast.14, ...), kind=kLoop, calls=%fused_computation.109 | loop fusion | flops 8388608 | bytes 4751360 | tf_op jit(solution)/shard_map/concatenate | solution.py:16
  137.3 0.8 copy-done.5
  138.5 0.9 copy-done.3
  139.8 0.9 copy-done.10
  141.3 0.9 copy-done.1
  143.3 0.9 copy-done.13
  145.1 0.7 copy-done.16
  146.3 0.5 convolution_multiply_fusion
  147.1 1.7 select_maximum_fusion
  148.8 3.6 %all-to-all-start.1 = ((f32[4,65,2048]{2,1,0:T(8,128)}), f32[4,65,2048]{2,1,0:T(8,128)S(1)}, u32[]{:S(2)}, u32[]{:S(2)}) async-start(f32[4,65,2048]{2,1,0:T(8,128)} %select_maximum_fusion), calls=%async_computation.1 | async-start | bytes 4718592 | tf_op jit(solution)/shard_map/all_to_all | solution.py:57
  152.4 1.4 copy.214
  153.9 1.0 reshape.187
  154.9 1.4 fusion.10
  159.3 2.1 copy.217
  161.4 2.5 mul.133
  163.9 17.1 %all-to-all-done.1 = f32[4,65,2048]{2,1,0:T(8,128)S(1)} async-done(((f32[4,65,2048]{2,1,0:T(8,128)}), f32[4,65,2048]{2,1,0:T(8,128)S(1)}, u32[]{:S(2)}, u32[]{:S(2)}) %all-to-all-start.1) | async-done | bytes 2129952 | tf_op jit(solution)/shard_map/all_to_all | solution.py:57
  181.0 3.5 %all-to-all-start.5 = ((f32[4,64,1152]{2,1,0:T(8,128)}), f32[4,64,1152]{2,1,0:T(8,128)S(1)}, u32[]{:S(2)}, u32[]{:S(2)}) async-start(f32[4,64,1152]{2,1,0:T(8,128)} %mul.133), calls=%async_computation.5 | async-start | bytes 2359296 | tf_op jit(solution)/shard_map/all_to_all | solution.py:41
  184.5 1.0 reduce_sum.57
  185.6 0.7 slice_reduce_fusion
  186.4 1.1 slice_bitcast_fusion
  187.5 1.1 select_maximum_fusion.1
  188.5 11.2 %all-to-all-done.5 = f32[4,64,1152]{2,1,0:T(8,128)S(1)} async-done(((f32[4,64,1152]{2,1,0:T(8,128)}), f32[4,64,1152]{2,1,0:T(8,128)S(1)}, u32[]{:S(2)}, u32[]{:S(2)}) %all-to-all-start.5) | async-done | bytes 1179680 | tf_op jit(solution)/shard_map/all_to_all | solution.py:41
  199.7 4.3 %all-to-all-start.2 = ((f32[8,9,2048]{2,1,0:T(8,128)}), f32[8,9,2048]{2,1,0:T(8,128)S(1)}, u32[]{:S(2)}, u32[]{:S(2)}) async-start(f32[8,9,2048]{2,1,0:T(8,128)} %select_maximum_fusion.1), calls=%async_computation.2 | async-start | bytes 2097152 | tf_op jit(solution)/shard_map/all_to_all | solution.py:66
  204.1 26.5 %all-to-all-done.2 = f32[8,9,2048]{2,1,0:T(8,128)S(1)} async-done(((f32[8,9,2048]{2,1,0:T(8,128)}), f32[8,9,2048]{2,1,0:T(8,128)S(1)}, u32[]{:S(2)}, u32[]{:S(2)}) %all-to-all-start.2) | async-done | bytes 589856 | tf_op jit(solution)/shard_map/all_to_all | solution.py:66
  230.6 1.1 tile.5
  231.7 3.5 %all-to-all-start.6 = ((f32[4,64,1152]{2,1,0:T(8,128)}), f32[4,64,1152]{2,1,0:T(8,128)S(1)}, u32[]{:S(2)}, u32[]{:S(2)}) async-start(f32[4,64,1152]{2,1,0:T(8,128)} %tile.5), calls=%async_computation.6 | async-start | bytes 2359296 | tf_op jit(solution)/shard_map/all_to_all | solution.py:35
  235.3 0.6 slice.354
  236.5 13.9 %all-to-all-done.6 = f32[4,64,1152]{2,1,0:T(8,128)S(1)} async-done(((f32[4,64,1152]{2,1,0:T(8,128)}), f32[4,64,1152]{2,1,0:T(8,128)S(1)}, u32[]{:S(2)}, u32[]{:S(2)}) %all-to-all-start.6) | async-done | bytes 1179680 | tf_op jit(solution)/shard_map/all_to_all | solution.py:35
  250.3 1.0 copy.346
  (105 shorter events, 14.8 us)
Async XLA Ops:
  7.2 1.0 copy-start.32
  7.2 66.0 %all-gather.2.cloned.1.call-start = ((), (), s32[]{:S(2)}) async-start(), calls=%async_computation.7 | async-start | bytes 5898240 | tf_op jit(solution)/shard_map/all_gather | solution.py:89
  8.2 23.8 %copy-start.28 = (bf16[1,128,2048]{2,1,0:T(8,128)(2,1)S(1)}, bf16[1,128,2048]{2,1,0:T(8,128)(2,1)}, u32[]{:S(2)}) copy-start(bf16[1,128,2048]{2,1,0:T(8,128)(2,1)} %param.10) | copy-start | bytes 1572868
  8.2 23.8 %copy-start.34 = (s32[1,128]{1,0:T(1,128)S(1)}, s32[1,128]{1,0:T(1,128)}, u32[]{:S(2)}) copy-start(s32[1,128]{1,0:T(1,128)} %param.11) | copy-start | bytes 1540
  32.0 0.7 copy-start.33
  32.9 14.0 %copy-start.15 = (bf16[1,128,2048]{2,1,0:T(8,128)(2,1)S(1)}, bf16[1,128,2048]{2,1,0:T(8,128)(2,1)}, u32[]{:S(2)}) copy-start(bf16[1,128,2048]{2,1,0:T(8,128)(2,1)} %param.15) | copy-start | bytes 1572868
  38.0 20.5 %all-to-all-start.4 = ((bf16[8,128,256]{2,1,0:T(8,128)(2,1)}), bf16[8,128,256]{2,1,0:T(8,128)(2,1)S(1)}, u32[]{:S(2)}, u32[]{:S(2)}) async-start(bf16[8,128,256]{2,1,0:T(8,128)(2,1)} %fusion.72), calls=%async_computation.4 | async-start | bytes 1048576 | tf_op jit(solution)/shard_map/all_to_all | solution.py:119
  43.1 5.0 %collective-permute-start = (bf16[4,2048]{1,0:T(4,128)(2,1)S(1)}, bf16[4,2048]{1,0:T(4,128)(2,1)S(1)}, u32[]{:S(2)}, u32[]{:S(2)}) collective-permute-start(bf16[4,2048]{1,0:T(4,128)(2,1)S(1)} %get-tuple-element.66), channel_id=1, source_target_pairs={{0,1},{1,2},{2,3},{3,4},{4,5},{5,6},{6,7},{8,9},{9,10},{10,11},{11... | collective-permute-start | bytes 49160 | tf_op jit(solution)/shard_map/ppermute | solution.py:18
  45.6 4.2 %collective-permute-start.1 = (bf16[4,2048]{1,0:T(4,128)(2,1)S(1)}, bf16[4,2048]{1,0:T(4,128)(2,1)S(1)}, u32[]{:S(2)}, u32[]{:S(2)}) collective-permute-start(bf16[4,2048]{1,0:T(4,128)(2,1)S(1)} %get-tuple-element.65), channel_id=1, source_target_pairs={{1,0},{2,1},{3,2},{4,3},{5,4},{6,5},{7,6},{9,8},{10,9},{11,10},{12... | collective-permute-start | bytes 49160 | tf_op jit(solution)/shard_map/ppermute | solution.py:20
  58.6 14.5 %copy-start.17 = (bf16[1024,2,128]{2,1,0:T(2,128)(2,1)}, bf16[1024,2,128]{2,1,0:T(2,128)(2,1)S(1)}, u32[]{:S(2)}) copy-start(bf16[1024,2,128]{2,1,0:T(2,128)(2,1)S(1)} %reshape_reshape.3) | copy-start | bytes 1572868
  83.6 19.2 %copy-start.25 = (bf16[16,16,8,128]{3,2,1,0:T(8,128)(2,1)S(1)}, bf16[16,16,8,128]{3,2,1,0:T(8,128)(2,1)}, u32[]{:S(2)}) copy-start(bf16[16,16,8,128]{3,2,1,0:T(8,128)(2,1)} %get-tuple-element.63) | copy-start | bytes 1572868
  102.8 2.0 copy-start.4
  102.8 2.0 copy-start.6
  102.8 2.0 copy-start.2
  102.8 3.4 %copy-start.9 = (bf16[16,128,1,128]{3,2,1,0:T(2,128)(2,1)}, bf16[16,128,1,128]{3,2,1,0:T(2,128)(2,1)S(1)}, u32[]{:S(2)}) copy-start(bf16[16,128,1,128]{3,2,1,0:T(2,128)(2,1)S(1)} %get-tuple-element.35) | copy-start | bytes 1572868
  102.8 4.4 %copy-start.8 = (bf16[16,128,1,128]{3,2,1,0:T(2,128)(2,1)}, bf16[16,128,1,128]{3,2,1,0:T(2,128)(2,1)S(1)}, u32[]{:S(2)}) copy-start(bf16[16,128,1,128]{3,2,1,0:T(2,128)(2,1)S(1)} %get-tuple-element.34) | copy-start | bytes 1572868
  102.8 5.0 %copy-start = (bf16[16,128,1,128]{3,2,1,0:T(2,128)(2,1)}, bf16[16,128,1,128]{3,2,1,0:T(2,128)(2,1)S(1)}, u32[]{:S(2)}) copy-start(bf16[16,128,1,128]{3,2,1,0:T(2,128)(2,1)S(1)} %get-tuple-element.33) | copy-start | bytes 1572868
  102.8 8.0 %copy-start.12 = (bf16[16,128,1,128]{3,2,1,0:T(2,128)(2,1)}, bf16[16,128,1,128]{3,2,1,0:T(2,128)(2,1)S(1)}, u32[]{:S(2)}) copy-start(bf16[16,128,1,128]{3,2,1,0:T(2,128)(2,1)S(1)} %get-tuple-element.30) | copy-start | bytes 1572868
  102.8 1.4 copy-start.24
  104.3 1.4 copy-start.23
  105.7 1.0 copy-start.22
  107.2 1.0 copy-start.21
  108.3 1.0 copy-start.20
  109.3 1.0 copy-start.19
  110.4 1.2 copy-start.27
  110.4 1.4 copy-start.29
  112.6 0.8 copy-start.14
  114.5 15.7 %collective-permute-start.2 = (bf16[4,2048]{0,1:T(8,128)(2,1)}, bf16[4,2048]{0,1:T(8,128)(2,1)}, u32[]{:S(2)}, u32[]{:S(2)}) collective-permute-start(bf16[4,2048]{0,1:T(8,128)(2,1)} %copy.192), channel_id=1, source_target_pairs={{1,0},{2,1},{3,2},{4,3},{5,4},{6,5},{7,6},{9,8},{10,9},{11,10},{12... | collective-permute-start | bytes 49160 | tf_op jit(solution)/shard_map/ppermute | solution.py:20
  116.8 13.4 %collective-permute-start.3 = (bf16[4,2048]{0,1:T(8,128)(2,1)}, bf16[4,2048]{0,1:T(8,128)(2,1)}, u32[]{:S(2)}, u32[]{:S(2)}) collective-permute-start(bf16[4,2048]{0,1:T(8,128)(2,1)} %copy.202), channel_id=1, source_target_pairs={{0,1},{1,2},{2,3},{3,4},{4,5},{5,6},{6,7},{8,9},{9,10},{10,11},{11... | collective-permute-start | bytes 49160 | tf_op jit(solution)/shard_map/ppermute | solution.py:18
  125.6 23.2 %all-to-all-start.3 = ((bf16[128,8,256]{0,2,1:T(8,128)(2,1)}), bf16[128,8,256]{0,2,1:T(8,128)(2,1)}, u32[]{:S(2)}, u32[]{:S(2)}) async-start(bf16[128,8,256]{0,2,1:T(8,128)(2,1)} %bitcast.33), calls=%async_computation.3 | async-start | bytes 1048576 | tf_op jit(solution)/shard_map/all_to_all | solution.py:122
  130.2 6.7 %copy-start.7 = (bf16[16,128,1,128]{3,2,1,0:T(2,128)(2,1)S(1)}, bf16[16,128,1,128]{3,2,1,0:T(2,128)(2,1)}, u32[]{:S(2)}) copy-start(bf16[16,128,1,128]{3,2,1,0:T(2,128)(2,1)} %copy-done.6) | copy-start | bytes 1572868
  136.9 1.2 copy-start.5
  138.2 1.2 copy-start.3
  139.4 1.2 copy-start.10
  139.4 1.5 copy-start.11
  140.9 1.2 copy-start.1
  142.9 1.2 copy-start.13
  144.8 1.0 copy-start.16
  146.3 0.8 copy-start.26
  148.8 32.2 %all-to-all-start.1 = ((f32[4,65,2048]{2,1,0:T(8,128)}), f32[4,65,2048]{2,1,0:T(8,128)S(1)}, u32[]{:S(2)}, u32[]{:S(2)}) async-start(f32[4,65,2048]{2,1,0:T(8,128)} %select_maximum_fusion), calls=%async_computation.1 | async-start | bytes 4718592 | tf_op jit(solution)/shard_map/all_to_all | solution.py:57
  152.4 2.5 copy-start.30
  154.9 1.4 copy-start.31
  156.6 1.0 copy-start.18
  181.0 18.7 %all-to-all-start.5 = ((f32[4,64,1152]{2,1,0:T(8,128)}), f32[4,64,1152]{2,1,0:T(8,128)S(1)}, u32[]{:S(2)}, u32[]{:S(2)}) async-start(f32[4,64,1152]{2,1,0:T(8,128)} %mul.133), calls=%async_computation.5 | async-start | bytes 2359296 | tf_op jit(solution)/shard_map/all_to_all | solution.py:41
  199.7 30.9 %all-to-all-start.2 = ((f32[8,9,2048]{2,1,0:T(8,128)}), f32[8,9,2048]{2,1,0:T(8,128)S(1)}, u32[]{:S(2)}, u32[]{:S(2)}) async-start(f32[8,9,2048]{2,1,0:T(8,128)} %select_maximum_fusion.1), calls=%async_computation.2 | async-start | bytes 2097152 | tf_op jit(solution)/shard_map/all_to_all | solution.py:66
  231.7 18.6 %all-to-all-start.6 = ((f32[4,64,1152]{2,1,0:T(8,128)}), f32[4,64,1152]{2,1,0:T(8,128)S(1)}, u32[]{:S(2)}, u32[]{:S(2)}) async-start(f32[4,64,1152]{2,1,0:T(8,128)} %tile.5), calls=%async_computation.6 | async-start | bytes 2359296 | tf_op jit(solution)/shard_map/all_to_all | solution.py:35
Sparse Core Ops, SparseCore 0:
  9.8 63.2 all-gather.1
